TPU v7x, 256 devices: a whole 4x4x8 slice. The times are simulated.
256 devices in a mesh: gx: 16 (over y, x), gy: 16 (over z, core).
Axes of the slice: x: 4, y: 4, z: 8, core: 2. Of those that a mesh axis runs over, the one named last changes fastest.
Arguments:
- state: float32 [6, 256, 49152], P(None, 'gx', 'gy'), as said below
- shock_height: float32 [256, 32], P('gx'), may hold values from 0.9 to 1.1
- wall_segment: int32 [256], P('gx'), may hold values from 0 to 15, never falling along the last dimension, each value on 1 to 32 neighbouring positions
- segment_level: int32 [16], replicated, may hold values from 0 to 15
- blow_table: float32 [16, 32], replicated, may hold values from 0.1 to 1.5
Outputs:
- state_new: float32 [6, 256, 49152], P(None, 'gx', 'gy')
- shock_new: float32 [256, 32], P('gx')
Inputs may be any that keep to these rules, and one draw needn't show every extreme that they name: `state`: each cell has density in [0.5, 2], p / density in [0.6, 2.5], q5 / density in [0.05, 0.6], u in [0, 2], v and w in [-1, 1]. `wall_segment`: segment numbers never fall along the stream; each segment covers 1 to 32 cells.
All inputs are finite; a program needn't handle non-finite values.
Results may differ from a plain program's by a relative error of at most 0.00002.
Values sent between devices are 32-bit elements; how exact they have to be, the bound alone decides.
No kernel may reach another device: no remote copies, remote signals or barrier semaphores. Data moves between devices by JAX's collectives and lax.ppermute only.
A program may use at most 64 MiB of HBM per device.

v0:
```python
import math
import jax
import jax.numpy as jnp
from jax import lax
from jax.sharding import PartitionSpec as P

HEAT_RATIO = 1.4
STREAM_STEP = 0.05
SPAN_STEP = 0.05
STRETCH_RATE = 2.0
CHARACTER_KELVIN = 3.0
WHITE_LAW_FACTOR = 1.0
LANDAU_TELLER = 0.002
FREE_PRESSURE = 0.1
FREE_MACH = 6.0
COURANT = 0.05


def padded(block, sides, width):
    for axis, dim in sides:
        count = lax.axis_size(axis)
        forward = [(i, i + 1) for i in range(count - 1)]
        backward = [(target, source) for source, target in forward]
        low = lax.ppermute(
            lax.slice_in_dim(block, block.shape[dim] - width, None, axis=dim), axis, forward
        )
        high = lax.ppermute(lax.slice_in_dim(block, 0, width, axis=dim), axis, backward)
        block = jnp.concatenate([low, block, high], axis=dim)
    return block


def broadcast(array, axis, root):
    mine = lax.axis_index(axis) == root
    return lax.psum(jnp.where(mine, array, jnp.zeros_like(array)), axis)


def zshift(values, offset, planes):
    length = values.shape[-1]
    plane_at = jnp.arange(length, dtype=jnp.int32) % planes
    if offset > 0:
        return jnp.where(
            plane_at >= offset,
            jnp.roll(values, offset, axis=-1),
            jnp.roll(values, offset - planes, axis=-1),
        )
    return jnp.where(
        plane_at < planes + offset,
        jnp.roll(values, offset, axis=-1),
        jnp.roll(values, offset + planes, axis=-1),
    )


def primitives(conserved):
    specific_volume_inverse = conserved[0]
    vel_x = conserved[1] / specific_volume_inverse
    vel_y = conserved[2] / specific_volume_inverse
    vel_z = conserved[3] / specific_volume_inverse
    thermodynamic_stress = (HEAT_RATIO - 1.0) * (
        conserved[4]
        - 0.5 * (conserved[1] * vel_x + conserved[2] * vel_y + conserved[3] * vel_z)
        - conserved[5]
    )
    sound_speed = jnp.sqrt(HEAT_RATIO * thermodynamic_stress / specific_volume_inverse)
    return (specific_volume_inverse, vel_x, vel_y, vel_z, thermodynamic_stress, sound_speed)


def face_difference(plus_flux, minus_flux, cells, axis_at, stride):

    def window(values, offset):
        return lax.slice_in_dim(
            values, offset * stride, (offset + cells + 1) * stride, axis=axis_at
        )

    upwind = (
        2.0 * window(plus_flux, 0)
        - 13.0 * window(plus_flux, 1)
        + 47.0 * window(plus_flux, 2)
        + 27.0 * window(plus_flux, 3)
        - 3.0 * window(plus_flux, 4)
    ) / 60.0
    downwind = (
        -3.0 * window(minus_flux, 1)
        + 27.0 * window(minus_flux, 2)
        + 47.0 * window(minus_flux, 3)
        - 13.0 * window(minus_flux, 4)
        + 2.0 * window(minus_flux, 5)
    ) / 60.0
    face_sum = upwind + downwind
    return lax.slice_in_dim(
        face_sum, stride, (cells + 1) * stride, axis=axis_at
    ) - lax.slice_in_dim(face_sum, 0, cells * stride, axis=axis_at)


def stretch(index_rows, total_rows):
    growth = jnp.exp(STRETCH_RATE * (index_rows + 0.5) / total_rows)
    denominator = math.exp(STRETCH_RATE) - 1.0
    return ((growth - 1.0) / denominator, STRETCH_RATE * growth / (total_rows * denominator))


def split_pair(fluxes, speeds, conserved):
    return (0.5 * (fluxes + speeds * conserved), 0.5 * (fluxes - speeds * conserved))


def stream_part(conserved_x, height_ext, spacing_rows, planes):
    columns = conserved_x.shape[1] - 6
    specific_volume_inverse, vel_x, vel_y, vel_z, thermodynamic_stress, sound_speed = primitives(
        conserved_x
    )
    metric = (
        SPAN_STEP
        * jnp.tile(height_ext, (1, conserved_x.shape[2] // planes))
        * spacing_rows[None, :]
    )
    fluxes = (
        jnp.stack(
            [
                conserved_x[1],
                conserved_x[1] * vel_x + thermodynamic_stress,
                conserved_x[2] * vel_x,
                conserved_x[3] * vel_x,
                (conserved_x[4] + thermodynamic_stress) * vel_x,
                conserved_x[5] * vel_x,
            ]
        )
        * metric
    )
    speeds = (jnp.abs(vel_x) + sound_speed) * metric
    plus_flux, minus_flux = split_pair(fluxes, speeds, conserved_x)
    return face_difference(plus_flux, minus_flux, columns, 1, 1)


def normal_part(conserved_y, slope_x, slope_z, shock_rate, eta_rows, planes):
    copies = conserved_y.shape[2] // planes
    row_count = copies - 6
    specific_volume_inverse, vel_x, vel_y, vel_z, thermodynamic_stress, sound_speed = primitives(
        conserved_y
    )
    face_area = STREAM_STEP * SPAN_STEP
    metric_x = -face_area * eta_rows[None, :] * jnp.tile(slope_x, (1, copies))
    metric_z = -face_area * eta_rows[None, :] * jnp.tile(slope_z, (1, copies))
    metric_t = -face_area * eta_rows[None, :] * jnp.tile(shock_rate, (1, copies))
    contra = metric_t + metric_x * vel_x + face_area * vel_y + metric_z * vel_z
    fluxes = jnp.stack(
        [
            conserved_y[0] * contra,
            conserved_y[1] * contra + metric_x * thermodynamic_stress,
            conserved_y[2] * contra + face_area * thermodynamic_stress,
            conserved_y[3] * contra + metric_z * thermodynamic_stress,
            (conserved_y[4] + thermodynamic_stress) * contra - metric_t * thermodynamic_stress,
            conserved_y[5] * contra,
        ]
    )
    speeds = jnp.abs(contra) + sound_speed * jnp.sqrt(
        metric_x * metric_x + face_area * face_area + metric_z * metric_z
    )
    plus_flux, minus_flux = split_pair(fluxes, speeds, conserved_y)
    return face_difference(plus_flux, minus_flux, row_count, 2, planes)


def span_part(conserved, height, spacing_rows, planes):
    specific_volume_inverse, vel_x, vel_y, vel_z, thermodynamic_stress, sound_speed = primitives(
        conserved
    )
    metric = (
        STREAM_STEP * jnp.tile(height, (1, conserved.shape[2] // planes)) * spacing_rows[None, :]
    )
    fluxes = (
        jnp.stack(
            [
                conserved[3],
                conserved[1] * vel_z,
                conserved[2] * vel_z,
                conserved[3] * vel_z + thermodynamic_stress,
                (conserved[4] + thermodynamic_stress) * vel_z,
                conserved[5] * vel_z,
            ]
        )
        * metric
    )
    speeds = (jnp.abs(vel_z) + sound_speed) * metric
    plus_flux, minus_flux = split_pair(fluxes, speeds, conserved)
    upwind = (
        2.0 * zshift(plus_flux, 2, planes)
        - 13.0 * zshift(plus_flux, 1, planes)
        + 47.0 * plus_flux
        + 27.0 * zshift(plus_flux, -1, planes)
        - 3.0 * zshift(plus_flux, -2, planes)
    ) / 60.0
    downwind = (
        -3.0 * zshift(minus_flux, 1, planes)
        + 27.0 * minus_flux
        + 47.0 * zshift(minus_flux, -1, planes)
        - 13.0 * zshift(minus_flux, -2, planes)
        + 2.0 * zshift(minus_flux, -3, planes)
    ) / 60.0
    face_sum = upwind + downwind
    return face_sum - zshift(face_sum, 1, planes)


def relaxation(conserved):
    specific_volume_inverse, vel_x, vel_y, vel_z, thermodynamic_stress, sound_speed = primitives(
        conserved
    )
    heavy_particle_kelvin = thermodynamic_stress / specific_volume_inverse
    oscillator_balanced_share = CHARACTER_KELVIN / (
        jnp.exp(CHARACTER_KELVIN / heavy_particle_kelvin) - 1.0
    )
    landau_teller_source = thermodynamic_stress / (
        LANDAU_TELLER * jnp.exp(WHITE_LAW_FACTOR * jnp.exp(-jnp.log(heavy_particle_kelvin) / 3.0))
    )
    return (
        specific_volume_inverse
        * (oscillator_balanced_share - conserved[5] / specific_volume_inverse)
        * landau_teller_source
    )


def slopes(height_ext, planes):
    columns = height_ext.shape[0] - 6
    slope_x = (
        height_ext[1 : columns + 1]
        - 8.0 * height_ext[2 : columns + 2]
        + 8.0 * height_ext[4 : columns + 4]
        - height_ext[5 : columns + 5]
    ) / (12.0 * STREAM_STEP)
    height = height_ext[3 : columns + 3]
    slope_z = (
        zshift(height, 2, planes)
        - 8.0 * zshift(height, 1, planes)
        + 8.0 * zshift(height, -1, planes)
        - zshift(height, -2, planes)
    ) / (12.0 * SPAN_STEP)
    return (slope_x, slope_z)


def shock_speed(top_row, slope_x, slope_z):
    specific_volume_inverse, vel_x, vel_y, vel_z, thermodynamic_stress, sound_speed = primitives(
        top_row
    )
    tilt_norm = jnp.sqrt(1.0 + slope_x * slope_x + slope_z * slope_z)
    normal = (vel_y - vel_x * slope_x - vel_z * slope_z) / tilt_norm
    sine_sq = slope_x * slope_x / (tilt_norm * tilt_norm)
    jump_pressure = FREE_PRESSURE * (
        1.0 + 2.0 * HEAT_RATIO / (HEAT_RATIO + 1.0) * (FREE_MACH * FREE_MACH * sine_sq - 1.0)
    )
    return tilt_norm * (
        normal + (jump_pressure - thermodynamic_stress) / (specific_volume_inverse * sound_speed)
    )


def wall_ghosts(first_rows, blowing, planes):
    mirror = jnp.concatenate(
        [
            first_rows[..., 2 * planes : 3 * planes],
            first_rows[..., planes : 2 * planes],
            first_rows[..., 0:planes],
        ],
        axis=-1,
    )
    blown_y = 2.0 * jnp.tile(blowing, (1, 3)) - mirror[2]
    stagnation_enthalpy_sum = (
        mirror[4] + 0.5 * (blown_y * blown_y - mirror[2] * mirror[2]) / mirror[0]
    )
    return jnp.stack([mirror[0], mirror[1], blown_y, mirror[3], stagnation_enthalpy_sum, mirror[5]])


def advance(
    conserved,
    conserved_x,
    conserved_y,
    height_ext,
    slope_x,
    slope_z,
    shock_rate,
    first_row,
    total_rows,
    planes,
):
    columns = conserved.shape[1]
    row_count = conserved.shape[2] // planes
    local_rows = (first_row + jnp.arange(row_count, dtype=jnp.int32)).astype(jnp.float32)
    eta_local, spacing_local = stretch(local_rows, total_rows)
    spacing_rows = jnp.repeat(spacing_local, planes)
    outer_rows = (first_row - 3 + jnp.arange(row_count + 6, dtype=jnp.int32)).astype(jnp.float32)
    eta_outer = stretch(outer_rows, total_rows)[0]
    eta_rows = jnp.repeat(eta_outer, planes)
    height = height_ext[3 : columns + 3]
    divergence = (
        stream_part(conserved_x, height_ext, spacing_rows, planes)
        + normal_part(conserved_y, slope_x, slope_z, shock_rate, eta_rows, planes)
        + span_part(conserved, height, spacing_rows, planes)
    )
    height_rows = jnp.tile(height, (1, row_count))
    rate_rows = jnp.tile(shock_rate, (1, row_count))
    volume = STREAM_STEP * SPAN_STEP * height_rows * spacing_rows[None, :]
    change = -divergence / volume - conserved * (rate_rows / height_rows)
    change = jnp.concatenate([change[:5], (change[5] + relaxation(conserved))[None]], axis=0)
    return conserved + COURANT / total_rows * change


def edge_fill(values, axis_at, cells, device_at, devices):
    positions = jnp.arange(cells + 6, dtype=jnp.int32)
    processor_arrangement = [1] * values.ndim
    processor_arrangement[axis_at] = cells + 6
    positions = positions.reshape(processor_arrangement)
    leading = lax.slice_in_dim(values, 3, 4, axis=axis_at)
    trailing = lax.slice_in_dim(values, cells + 2, cells + 3, axis=axis_at)
    values = jnp.where((device_at == 0) & (positions < 3), leading, values)
    return jnp.where((device_at == devices - 1) & (positions >= cells + 3), trailing, values)


def wall_flux(wall_segment, segment_level, blow_table):
    seg_hit = wall_segment[:, None] == jnp.arange(segment_level.shape[0], dtype=jnp.int32)[None, :]
    levels = jnp.sum(jnp.where(seg_hit, segment_level[None, :], 0), axis=1)
    level_hit = levels[:, None] == jnp.arange(blow_table.shape[0], dtype=jnp.int32)[None, :]
    return jnp.sum(jnp.where(level_hit[:, :, None], blow_table[None, :, :], 0.0), axis=1)


def shards(state, shock_height, wall_segment, segment_level, blow_table):
    planes = blow_table.shape[1]
    columns = state.shape[1]
    length = state.shape[2]
    row_count = length // planes
    col_devs = lax.axis_size("gx")
    row_devs = lax.axis_size("gy")
    col_dev = lax.axis_index("gx")
    row_dev = lax.axis_index("gy")
    total_rows = row_count * row_devs
    conserved_x = padded(state, (("gx", 1),), 3)
    height_ext = padded(shock_height, (("gx", 0),), 3)
    conserved_x = edge_fill(conserved_x, 1, columns, col_dev, col_devs)
    height_ext = edge_fill(height_ext, 0, columns, col_dev, col_devs)
    slope_x, slope_z = slopes(height_ext, planes)
    own_rate = shock_speed(state[:, :, length - planes :], slope_x, slope_z)
    shock_rate = broadcast(own_rate, "gy", row_devs - 1)
    blowing = wall_flux(wall_segment, segment_level, blow_table)
    halo_y = padded(state, (("gy", 2),), 3 * planes)
    ghost_below = jnp.where(
        row_dev == 0,
        wall_ghosts(state[..., : 3 * planes], blowing, planes),
        halo_y[..., : 3 * planes],
    )
    ghost_above = jnp.where(
        row_dev == row_devs - 1,
        jnp.tile(state[..., length - planes :], (1, 1, 3)),
        halo_y[..., length + 3 * planes :],
    )
    conserved_y = jnp.concatenate([ghost_below, state, ghost_above], axis=2)
    state_new = advance(
        state,
        conserved_x,
        conserved_y,
        height_ext,
        slope_x,
        slope_z,
        shock_rate,
        row_dev * row_count,
        total_rows,
        planes,
    )
    shock_new = shock_height + COURANT / total_rows * shock_rate
    return (state_new, shock_new)


def solution(mesh):
    in_specs = (P(None, "gx", "gy"), P("gx", None), P("gx"), P(), P())
    out_specs = (P(None, "gx", "gy"), P("gx", None))
    return jax.shard_map(shards, mesh=mesh, in_specs=in_specs, out_specs=out_specs, check_vma=False)
```

profile of v0, /device:TPU:8, one launch (start us, length us, event | category | flops | bytes accessed | tf_op | source)
XLA Modules:
  0.0 124.9 jit_solution(7692212084763646776)
XLA Ops:
  0.7 0.8 fusion.104
  1.5 3.4 %collective-permute-start.2 = (f32[3,32]{1,0:T(4,128)S(1)}, f32[3,32]{1,0:T(4,128)S(1)}, u32[]{:S(2)}, u32[]{:S(2)}) collective-permute-start(f32[3,32]{1,0:T(4,128)S(1)} %get-tuple-element.71), channel_id=1, source_target_pairs={{0,16},{16,32},{32,48},{48,64},{64,80},{80,96},{96,112},{112,128},... | collective-permute-start | bytes 1160 | tf_op jit(solution)/shard_map/ppermute | solution.py:24
  4.9 4.6 %collective-permute-start.3 = (f32[3,32]{1,0:T(4,128)S(1)}, f32[3,32]{1,0:T(4,128)S(1)}, u32[]{:S(2)}, u32[]{:S(2)}) collective-permute-start(f32[3,32]{1,0:T(4,128)S(1)} %get-tuple-element.72), channel_id=1, source_target_pairs={{16,0},{32,16},{48,32},{64,48},{80,64},{96,80},{112,96},{128,112},... | collective-permute-start | bytes 1160 | tf_op jit(solution)/shard_map/ppermute | solution.py:27
  9.4 2.2 %fusion.97 = (f32[6,3,3072]{2,1,0:T(4,128)}, f32[6,3,3072]{2,1,0:T(4,128)}) fusion(f32[6,16,3072]{2,1,0:T(8,128)} %param.5), kind=kLoop, calls=%fused_computation.217 | loop fusion | bytes 884736 | tf_op jit(solution)/shard_map/slice | solution.py:25
  11.6 1.9 %collective-permute-start = (f32[6,3,3072]{2,1,0:T(4,128)}, f32[6,3,3072]{2,1,0:T(4,128)}, u32[]{:S(2)}, u32[]{:S(2)}) collective-permute-start(f32[6,3,3072]{2,1,0:T(4,128)} %get-tuple-element.50), channel_id=1, source_target_pairs={{0,16},{16,32},{32,48},{48,64},{64,80},{80,96},{96,112},{112,128},... | collective-permute-start | bytes 663560 | tf_op jit(solution)/shard_map/ppermute | solution.py:24
  13.5 6.0 %collective-permute-start.1 = (f32[6,3,3072]{2,1,0:T(4,128)}, f32[6,3,3072]{2,1,0:T(4,128)}, u32[]{:S(2)}, u32[]{:S(2)}) collective-permute-start(f32[6,3,3072]{2,1,0:T(4,128)} %get-tuple-element.51), channel_id=1, source_target_pairs={{16,0},{32,16},{48,32},{64,48},{80,64},{96,80},{112,96},{128,112},... | collective-permute-start | bytes 663560 | tf_op jit(solution)/shard_map/ppermute | solution.py:27
  19.6 0.7 fusion.98
  20.3 1.9 %collective-permute-start.4 = (f32[6,16,96]{2,1,0:T(8,128)}, f32[6,16,96]{2,1,0:T(8,128)}, u32[]{:S(2)}, u32[]{:S(2)}) collective-permute-start(f32[6,16,96]{2,1,0:T(8,128)} %get-tuple-element.53), channel_id=1, source_target_pairs={{0,1},{1,2},{2,3},{3,4},{4,5},{5,6},{6,7},{7,8},{8,9},{9,10},{10,1... | collective-permute-start | bytes 110600 | tf_op jit(solution)/shard_map/ppermute | solution.py:24
  26.3 0.7 copy_bitcast_fusion
  27.8 0.7 tile.39
  28.6 0.7 mul.830
  29.3 1.3 %collective-permute-start.5 = (f32[6,16,96]{2,1,0:T(8,128)}, f32[6,16,96]{2,1,0:T(8,128)}, u32[]{:S(2)}, u32[]{:S(2)}) collective-permute-start(f32[6,16,96]{2,1,0:T(8,128)} %get-tuple-element.52), channel_id=1, source_target_pairs={{1,0},{2,1},{3,2},{4,3},{5,4},{6,5},{7,6},{8,7},{9,8},{10,9},{11,1... | collective-permute-start | bytes 110600 | tf_op jit(solution)/shard_map/ppermute | solution.py:27
  33.4 1.1 tile.92
  34.5 1.0 tile.93
  35.5 1.5 %fusion.79 = (f32[16,32]{1,0:T(8,128)S(1)}, f32[16,32]{1,0:T(8,128)}, f32[16,32]{1,0:T(8,128)}) fusion(f32[6,16,3072]{2,1,0:T(8,128)S(1)} %copy-done, pred[]{:T(512)S(6)} %eq.69, f32[22,32]{1,0:T(8,128)S(1)} %fusion.56, f32[16,2]{1,0:T(8,128)} %get-tuple-element.62, f32[16,30]{1,0:T(8,128)} %get-tuple-element.64, f32[16,1]{1,0:T(8,128)} %get-tuple-element.66, ...), kind=kLoop, calls=%fused_computation.193 | loop fusion | flops 26624 | bytes 34817 | tf_op jit(solution)/shard_map/jit(_where)/select_n | solution.py:34
  37.0 31.8 %psum.7 = f32[16,32]{1,0:T(8,128)} all-reduce(f32[16,32]{1,0:T(8,128)S(1)} %get-tuple-element.12), channel_id=1, replica_groups=mesh['gx'=16,'gy'=16] {'gy'}, use_global_device_ids=true, to_apply=%region_2.3 | all-reduce | flops 512 | bytes 4096 | tf_op jit(solution)/shard_map/psum | solution.py:34
  68.9 0.7 tile.94
  69.6 1.1 tile.95
  70.7 1.1 multiply_dynamic-update-slice_fusion.7
  71.9 0.9 broadcast_multiply_fusion.3
  73.5 1.8 %fusion.85 = (f32[6,16,3041]{2,1,0:T(8,128)}, f32[6,16,3041]{2,1,0:T(8,128)}) fusion(f32[6,16,3072]{2,1,0:T(8,128)S(1)} %get-tuple-element.19), kind=kLoop, calls=%fused_computation.205 | loop fusion | bytes 4670976 | tf_op jit(solution)/shard_map/jit(_roll_static)/slice | solution.py:49
  75.2 1.8 %fusion.86 = (f32[6,16,3071]{2,1,0:T(8,128)}, f32[6,16,3071]{2,1,0:T(8,128)}) fusion(f32[6,16,3072]{2,1,0:T(8,128)S(1)} %get-tuple-element.19), kind=kLoop, calls=%fused_computation.206 | loop fusion | bytes 4717056 | tf_op jit(solution)/shard_map/jit(_roll_static)/slice | solution.py:48
  77.1 1.8 %fusion.89 = (f32[6,16,3042]{2,1,0:T(8,128)}, f32[6,16,3042]{2,1,0:T(8,128)}) fusion(f32[6,16,3072]{2,1,0:T(8,128)S(1)} %get-tuple-element.20), kind=kLoop, calls=%fused_computation.209 | loop fusion | bytes 4672512 | tf_op jit(solution)/shard_map/jit(_roll_static)/slice | solution.py:49
  78.9 1.8 %fusion.90 = (f32[6,16,3070]{2,1,0:T(8,128)}, f32[6,16,3070]{2,1,0:T(8,128)}) fusion(f32[6,16,3072]{2,1,0:T(8,128)S(1)} %get-tuple-element.20), kind=kLoop, calls=%fused_computation.210 | loop fusion | bytes 4715520 | tf_op jit(solution)/shard_map/jit(_roll_static)/slice | solution.py:48
  80.7 1.9 %fusion.93 = (f32[6,16,3041]{2,1,0:T(8,128)}, f32[6,16,3041]{2,1,0:T(8,128)}) fusion(f32[6,16,3072]{2,1,0:T(8,128)S(1)} %get-tuple-element.20), kind=kLoop, calls=%fused_computation.213 | loop fusion | bytes 4670976 | tf_op jit(solution)/shard_map/jit(_roll_static)/slice | solution.py:49
  82.5 1.8 %fusion.94 = (f32[6,16,3071]{2,1,0:T(8,128)}, f32[6,16,3071]{2,1,0:T(8,128)}) fusion(f32[6,16,3072]{2,1,0:T(8,128)S(1)} %get-tuple-element.20), kind=kLoop, calls=%fused_computation.214 | loop fusion | bytes 4717056 | tf_op jit(solution)/shard_map/jit(_roll_static)/slice | solution.py:48
  84.3 1.4 %slice.663 = f32[6,16,3070]{2,1,0:T(8,128)} slice(f32[6,16,3072]{2,1,0:T(8,128)S(1)} %get-tuple-element.19), slice={[0:6], [0:16], [2:3072]} | slice | bytes 2357760 | tf_op jit(solution)/shard_map/jit(_roll_static)/slice | solution.py:48
  85.7 1.4 %slice.667 = f32[6,16,3069]{2,1,0:T(8,128)} slice(f32[6,16,3072]{2,1,0:T(8,128)S(1)} %get-tuple-element.19), slice={[0:6], [0:16], [3:3072]} | slice | bytes 2356992 | tf_op jit(solution)/shard_map/jit(_roll_static)/slice | solution.py:48
  87.1 0.7 fusion.84
  87.8 0.7 fusion.87
  88.5 0.7 fusion.88
  89.2 0.7 fusion.91
  90.6 0.7 fusion.95
  91.3 0.7 slice.665
  92.6 0.7 slice.669
  93.4 1.2 tile.35
  94.7 1.7 %broadcast_multiply_fusion.2 = f32[22,3072]{1,0:T(8,128)} fusion(f32[22,3072]{1,0:T(8,128)} %tile.35, f32[3072]{0:T(1024)S(1)} %copy-done.18), kind=kLoop, calls=%fused_computation.132 | loop fusion | flops 67584 | bytes 552960 | tf_op jit(solution)/shard_map/mul | solution.py:110
  96.4 8.5 %fusion.32 = f32[6,16,3072]{2,1,0:T(8,128)S(1)} fusion(f32[6,16,3070]{2,1,0:T(8,128)} %get-tuple-element.37, f32[6,16,2]{2,1,0:T(8,128)} %get-tuple-element.39, f32[6,16,30]{2,1,0:T(8,128)} %get-tuple-element.33, f32[6,16,3042]{2,1,0:T(8,128)} %get-tuple-element.35, f32[6,16,3071]{2,1,0:T(8,128)} %get-tuple-element.45, f32[6,16,1]{2,1,0:T(8,128)} %get-tuple-element.47, ...), kind=kLoop, calls=%fused_computation.60 | loop fusion | flops 14155776 | bytes 22821888 | tf_op jit(solution)/shard_map/add | solution.py:196
  105.6 1.4 %slice.673 = f32[6,16,3041]{2,1,0:T(8,128)} slice(f32[6,16,3072]{2,1,0:T(8,128)S(1)} %fusion.32), slice={[0:6], [0:16], [31:3072]} | slice | bytes 2335488 | tf_op jit(solution)/shard_map/jit(_roll_static)/slice | solution.py:44
  109.4 0.8 broadcast_select_fusion
  110.9 1.7 %concatenate.126 = f32[6,16,3264]{2,1,0:T(8,128)S(1)} concatenate(f32[6,16,96]{2,1,0:T(8,128)} %broadcast_select_fusion.1, f32[6,16,3072]{2,1,0:T(8,128)S(1)} %copy-done, f32[6,16,96]{2,1,0:T(8,128)S(1)} %broadcast_select_fusion), dimensions={2} | concatenate | bytes 2506752 | tf_op jit(solution)/shard_map/concatenate | solution.py:348
  113.6 2.3 %fusion.13 = f32[6,16,3104]{2,1,0:T(8,128)S(1)} fusion(f32[6,16,3264]{2,1,0:T(8,128)S(1)} %get-tuple-element.18, f32[6,16,3264]{2,1,0:T(8,128)S(1)} %get-tuple-element.17), kind=kLoop, calls=%fused_computation.29 | loop fusion | flops 5959680 | bytes 13111296 | tf_op jit(solution)/shard_map/add | solution.py:88
  115.9 1.4 %fusion.10 = f32[6,22,3072]{2,1,0:T(8,128)S(1)} fusion(f32[6,3,3072]{2,1,0:T(4,128)} %collective-permute-done.1, f32[6,16,3072]{2,1,0:T(8,128)S(1)} %copy-done, f32[6,3,3072]{2,1,0:T(4,128)} %collective-permute-done, f32[6,3072]{1,0:T(8,128)S(1)} %copy-done.15, f32[6,3072]{1,0:T(8,128)S(1)} %copy-done.16, pred[22]{0:T(512)(128)(4,1)S(1)} %copy-done.37, ...), kind=kLoop, calls=%fused_computation.21 | loop fusion | flops 1622016 | bytes 3391532 | tf_op jit(solution)/shard_map/jit(_where)/select_n | solution.py:309
  117.9 0.9 copy-done.9
  119.3 2.2 %fusion.2 = f32[6,17,3072]{2,1,0:T(8,128)S(1)} fusion(f32[6,22,3072]{2,1,0:T(8,128)S(1)} %get-tuple-element.16, f32[6,22,3072]{2,1,0:T(8,128)S(1)} %get-tuple-element.15), kind=kLoop, calls=%fused_computation.3 | loop fusion | flops 6266880 | bytes 13787136 | tf_op jit(solution)/shard_map/add | solution.py:88
  121.6 0.9 fusion.25
  122.6 0.8 copy-done.8
  123.7 1.2 fusion.45
  (160 shorter events, 15.6 us)
Async XLA Ops:
  0.6 21.5 %copy-start.24 = (f32[16,32]{1,0:T(8,128)S(1)}, f32[16,32]{1,0:T(8,128)}, u32[]{:S(2)}) copy-start(f32[16,32]{1,0:T(8,128)} %param.6) | copy-start | bytes 6148
  0.6 18.9 %copy-start = (f32[6,16,3072]{2,1,0:T(8,128)S(1)}, f32[6,16,3072]{2,1,0:T(8,128)}, u32[]{:S(2)}) copy-start(f32[6,16,3072]{2,1,0:T(8,128)} %param.5) | copy-start | bytes 3538948
  1.5 27.8 %collective-permute-start.2 = (f32[3,32]{1,0:T(4,128)S(1)}, f32[3,32]{1,0:T(4,128)S(1)}, u32[]{:S(2)}, u32[]{:S(2)}) collective-permute-start(f32[3,32]{1,0:T(4,128)S(1)} %get-tuple-element.71), channel_id=1, source_target_pairs={{0,16},{16,32},{32,48},{48,64},{64,80},{80,96},{96,112},{112,128},... | collective-permute-start | bytes 1160 | tf_op jit(solution)/shard_map/ppermute | solution.py:24
  4.9 25.7 %collective-permute-start.3 = (f32[3,32]{1,0:T(4,128)S(1)}, f32[3,32]{1,0:T(4,128)S(1)}, u32[]{:S(2)}, u32[]{:S(2)}) collective-permute-start(f32[3,32]{1,0:T(4,128)S(1)} %get-tuple-element.72), channel_id=1, source_target_pairs={{16,0},{32,16},{48,32},{64,48},{80,64},{96,80},{112,96},{128,112},... | collective-permute-start | bytes 1160 | tf_op jit(solution)/shard_map/ppermute | solution.py:27
  11.6 104.3 %collective-permute-start = (f32[6,3,3072]{2,1,0:T(4,128)}, f32[6,3,3072]{2,1,0:T(4,128)}, u32[]{:S(2)}, u32[]{:S(2)}) collective-permute-start(f32[6,3,3072]{2,1,0:T(4,128)} %get-tuple-element.50), channel_id=1, source_target_pairs={{0,16},{16,32},{32,48},{48,64},{64,80},{80,96},{96,112},{112,128},... | collective-permute-start | bytes 663560 | tf_op jit(solution)/shard_map/ppermute | solution.py:24
  13.5 102.4 %collective-permute-start.1 = (f32[6,3,3072]{2,1,0:T(4,128)}, f32[6,3,3072]{2,1,0:T(4,128)}, u32[]{:S(2)}, u32[]{:S(2)}) collective-permute-start(f32[6,3,3072]{2,1,0:T(4,128)} %get-tuple-element.51), channel_id=1, source_target_pairs={{16,0},{32,16},{48,32},{64,48},{80,64},{96,80},{112,96},{128,112},... | collective-permute-start | bytes 663560 | tf_op jit(solution)/shard_map/ppermute | solution.py:27
  20.3 90.0 %collective-permute-start.4 = (f32[6,16,96]{2,1,0:T(8,128)}, f32[6,16,96]{2,1,0:T(8,128)}, u32[]{:S(2)}, u32[]{:S(2)}) collective-permute-start(f32[6,16,96]{2,1,0:T(8,128)} %get-tuple-element.53), channel_id=1, source_target_pairs={{0,1},{1,2},{2,3},{3,4},{4,5},{5,6},{6,7},{7,8},{8,9},{9,10},{10,1... | collective-permute-start | bytes 110600 | tf_op jit(solution)/shard_map/ppermute | solution.py:24
  22.8 73.6 %copy-start.29 = (pred[3072]{0:T(1024)(128)(4,1)}, pred[3072]{0:T(1024)(128)(4,1)S(1)}, u32[]{:S(2)}) copy-start(pred[3072]{0:T(1024)(128)(4,1)S(1)} %get-tuple-element.82) | copy-start | bytes 9220
  25.0 0.7 copy-start.40
  25.0 0.7 copy-start.41
  25.0 0.9 copy-start.35
  25.2 45.5 %copy-start.7 = (f32[1,16,3072]{2,1,0:T(8,128)}, f32[1,16,3072]{2,1,0:T(8,128)S(1)}, u32[]{:S(2)}) copy-start(f32[1,16,3072]{2,1,0:T(8,128)S(1)} %get-tuple-element.3) | copy-start | bytes 589828
  26.2 7.1 %copy-start.22 = (f32[6,16,96]{2,1,0:T(8,128)}, f32[6,16,96]{2,1,0:T(8,128)S(1)}, u32[]{:S(2)}) copy-start(f32[6,16,96]{2,1,0:T(8,128)S(1)} %constant_dynamic-update-slice_fusion) | copy-start | bytes 110596
  26.3 7.1 %copy-start.36 = (pred[22]{0:T(512)(128)(4,1)}, pred[22]{0:T(512)(128)(4,1)S(1)}, u32[]{:S(2)}) copy-start(pred[22]{0:T(512)(128)(4,1)S(1)} %get-tuple-element.73) | copy-start | bytes 70
  26.3 7.1 %copy-start.38 = (pred[22]{0:T(512)(128)(4,1)}, pred[22]{0:T(512)(128)(4,1)S(1)}, u32[]{:S(2)}) copy-start(pred[22]{0:T(512)(128)(4,1)S(1)} %get-tuple-element.74) | copy-start | bytes 70
  29.3 79.7 %collective-permute-start.5 = (f32[6,16,96]{2,1,0:T(8,128)}, f32[6,16,96]{2,1,0:T(8,128)}, u32[]{:S(2)}, u32[]{:S(2)}) collective-permute-start(f32[6,16,96]{2,1,0:T(8,128)} %get-tuple-element.52), channel_id=1, source_target_pairs={{1,0},{2,1},{3,2},{4,3},{5,4},{6,5},{7,6},{8,7},{9,8},{10,9},{11,1... | collective-permute-start | bytes 110600 | tf_op jit(solution)/shard_map/ppermute | solution.py:27
  70.7 1.2 copy-start.10
  70.7 1.2 copy-start.11
  70.7 1.2 copy-start.17
  70.7 1.2 copy-start.26
  71.8 1.2 copy-start.5
  71.9 1.2 copy-start.3
  72.8 0.7 copy-start.6
  93.3 1.3 %copy-start.18 = (f32[3072]{0:T(1024)S(1)}, f32[3072]{0:T(1024)}, u32[]{:S(2)}) copy-start(f32[3072]{0:T(1024)} %mul.794) | copy-start | bytes 36868
  93.4 3.0 %copy-start.31 = (pred[3072]{0:T(1024)(128)(4,1)S(1)}, pred[3072]{0:T(1024)(128)(4,1)}, u32[]{:S(2)}) copy-start(pred[3072]{0:T(1024)(128)(4,1)} %get-tuple-element.81) | copy-start | bytes 9220
  93.4 3.0 %copy-start.32 = (pred[3072]{0:T(1024)(128)(4,1)S(1)}, pred[3072]{0:T(1024)(128)(4,1)}, u32[]{:S(2)}) copy-start(pred[3072]{0:T(1024)(128)(4,1)} %get-tuple-element.79) | copy-start | bytes 9220
  93.4 2.9 %copy-start.33 = (pred[3072]{0:T(1024)(128)(4,1)S(1)}, pred[3072]{0:T(1024)(128)(4,1)}, u32[]{:S(2)}) copy-start(pred[3072]{0:T(1024)(128)(4,1)} %get-tuple-element.80) | copy-start | bytes 9220
  93.4 2.9 %copy-start.34 = (pred[3072]{0:T(1024)(128)(4,1)S(1)}, pred[3072]{0:T(1024)(128)(4,1)}, u32[]{:S(2)}) copy-start(pred[3072]{0:T(1024)(128)(4,1)} %fusion.63) | copy-start | bytes 9220
  96.4 8.6 %copy-start.21 = (f32[16,32]{1,0:T(8,128)S(1)}, f32[16,32]{1,0:T(8,128)}, u32[]{:S(2)}) copy-start(f32[16,32]{1,0:T(8,128)} %psum.7) | copy-start | bytes 6148
  96.4 8.6 %copy-start.25 = (f32[16,32]{1,0:T(8,128)S(1)}, f32[16,32]{1,0:T(8,128)}, u32[]{:S(2)}) copy-start(f32[16,32]{1,0:T(8,128)} %param.6) | copy-start | bytes 6148
  105.0 2.1 %copy-start.1 = (f32[6,16,3072]{2,1,0:T(8,128)}, f32[6,16,3072]{2,1,0:T(8,128)S(1)}, u32[]{:S(2)}) copy-start(f32[6,16,3072]{2,1,0:T(8,128)S(1)} %fusion.32) | copy-start | bytes 3538948
  107.6 0.7 copy-start.28
  107.9 0.7 copy-start.27
  108.6 0.8 copy-start.20
  108.6 1.6 %copy-start.23 = (f32[6,16,96]{2,1,0:T(8,128)S(1)}, f32[6,16,96]{2,1,0:T(8,128)}, u32[]{:S(2)}) copy-start(f32[6,16,96]{2,1,0:T(8,128)} %copy-done.22) | copy-start | bytes 110596
  110.9 1.7 %copy-start.14 = (f32[3264]{0:T(1024)S(1)}, f32[3264]{0:T(1024)}, u32[]{:S(2)}) copy-start(f32[3264]{0:T(1024)} %mul.830) | copy-start | bytes 39172
  113.5 2.3 %copy-start.15 = (f32[6,3072]{1,0:T(8,128)S(1)}, f32[6,3072]{1,0:T(8,128)}, u32[]{:S(2)}) copy-start(f32[6,3072]{1,0:T(8,128)} %get-tuple-element.77) | copy-start | bytes 221188
  113.5 2.3 %copy-start.16 = (f32[6,3072]{1,0:T(8,128)S(1)}, f32[6,3072]{1,0:T(8,128)}, u32[]{:S(2)}) copy-start(f32[6,3072]{1,0:T(8,128)} %get-tuple-element.78) | copy-start | bytes 221188
  113.5 2.3 %copy-start.37 = (pred[22]{0:T(512)(128)(4,1)S(1)}, pred[22]{0:T(512)(128)(4,1)}, u32[]{:S(2)}) copy-start(pred[22]{0:T(512)(128)(4,1)} %copy-done.36) | copy-start | bytes 70
  113.6 2.3 %copy-start.39 = (pred[22]{0:T(512)(128)(4,1)S(1)}, pred[22]{0:T(512)(128)(4,1)}, u32[]{:S(2)}) copy-start(pred[22]{0:T(512)(128)(4,1)} %copy-done.38) | copy-start | bytes 70
  115.9 1.5 %copy-start.19 = (f32[3072]{0:T(1024)S(1)}, f32[3072]{0:T(1024)}, u32[]{:S(2)}) copy-start(f32[3072]{0:T(1024)} %mul.794) | copy-start | bytes 36868
  117.8 1.0 copy-start.9
  119.3 2.3 %copy-start.2 = (f32[6,16,3072]{2,1,0:T(8,128)S(1)}, f32[6,16,3072]{2,1,0:T(8,128)}, u32[]{:S(2)}) copy-start(f32[6,16,3072]{2,1,0:T(8,128)} %copy-done.1) | copy-start | bytes 3538948
  119.3 2.3 %copy-start.4 = (f32[6,16,3041]{2,1,0:T(8,128)S(1)}, f32[6,16,3041]{2,1,0:T(8,128)}, u32[]{:S(2)}) copy-start(f32[6,16,3041]{2,1,0:T(8,128)} %slice.673) | copy-start | bytes 3503236
  119.3 2.3 %copy-start.12 = (f32[16,3072]{1,0:T(8,128)S(1)}, f32[16,3072]{1,0:T(8,128)}, u32[]{:S(2)}) copy-start(f32[16,3072]{1,0:T(8,128)} %get-tuple-element.58) | copy-start | bytes 589828
  119.3 2.3 %copy-start.13 = (f32[16,3072]{1,0:T(8,128)S(1)}, f32[16,3072]{1,0:T(8,128)}, u32[]{:S(2)}) copy-start(f32[16,3072]{1,0:T(8,128)} %get-tuple-element.59) | copy-start | bytes 589828
  119.3 2.3 %copy-start.30 = (pred[3072]{0:T(1024)(128)(4,1)S(1)}, pred[3072]{0:T(1024)(128)(4,1)}, u32[]{:S(2)}) copy-start(pred[3072]{0:T(1024)(128)(4,1)} %copy-done.29) | copy-start | bytes 9220
  122.5 0.9 copy-start.8
where the time goes:
time: 126 us; the launch traced here: 125 us
  local copies, waits for them, and re-layouts  43.7 us (35%)
  blocking collectives  31.8 us (25%)
  other arithmetic  28.7 us (23%)
  starting transfers between devices  19.1 us (15%)
  between operations  1.58 us (1%)
    psum x1, blocking collectives, broadcast(): return lax.psum(jnp.where(mine, array, jnp.zeros_like(array)), axis)  31.8 us
    slice x15, local copies, waits for them, and re-layouts, zshift(): jnp.roll(values, offset, axis=-1)  13.7 us
    ppermute x3, starting transfers between devices, padded(): lax.ppermute(lax.slice_in_dim(block, 0, width, axis=dim), axis, backward)  11.9 us
    slice x8, local copies, waits for them, and re-layouts, zshift(): jnp.roll(values, offset + planes, axis=-1)  8.92 us
    add x1, other arithmetic, span_part(): face_sum = upwind + downwind  8.53 us
    ppermute x3, starting transfers between devices, padded(): lax.ppermute(lax.slice_in_dim(block, block.shape[dim] - width, None, axis...  7.2 us
    add x2, other arithmetic, face_difference(): face_sum = upwind + downwind  4.5 us
    unnamed x87, local copies, waits for them, and re-layouts  3.51 us
  transfers between devices with their start and end apart: 6, of which 0 were waited for; matrix products, arithmetic and copies ran while one was open for 49% of the time, Pallas kernels for 0%

commit v1 on v0

--- a/solution.py
+++ b/solution.py
@@ -31,7 +31,7 @@
 
 def broadcast(array, axis, root):
     mine = lax.axis_index(axis) == root
-    return lax.psum(jnp.where(mine, array, jnp.zeros_like(array)), axis)
+    return jnp.sum(lax.all_gather(jnp.where(mine, array, jnp.zeros_like(array)), axis), axis=0)
 
 
 def zshift(values, offset, planes):

time: 126 us -> 118 us (0.937)
  blocking collectives: 31.8 us -> 22.7 us
    psum x1 -> x0, blocking collectives: 31.8 us -> none  [broadcast(): return lax.psum(jnp.where(mine, array, jnp.zeros_like(array)), axis)]
    all_gather x0 -> x1, blocking collectives: none -> 22.7 us  [broadcast(): lax.all_gather(jnp.where(mine, array, jnp.zeros_like(array)), axis)]
  transfers between devices with their start and end apart: 6 -> 6, of which waited for: 0 -> 0; matrix products, arithmetic and copies ran while one was open for 49% -> 53% of each run, Pallas kernels for 0% -> 0%
where the time goes in v1:
time: 118 us; the launch traced here: 116 us
  local copies, waits for them, and re-layouts  43.5 us (37%)
  other arithmetic  29.5 us (25%)
  blocking collectives  22.7 us (19%)
  starting transfers between devices  19.1 us (16%)
  between operations  1.58 us (1%)
    all_gather x1, blocking collectives, broadcast(): lax.all_gather(jnp.where(mine, array, jnp.zeros_like(array)), axis)  22.7 us
    slice x15, local copies, waits for them, and re-layouts, zshift(): jnp.roll(values, offset, axis=-1)  13.7 us
    ppermute x3, starting transfers between devices, padded(): lax.ppermute(lax.slice_in_dim(block, 0, width, axis=dim), axis, backward)  11.9 us
    slice x8, local copies, waits for them, and re-layouts, zshift(): jnp.roll(values, offset + planes, axis=-1)  8.92 us
    add x1, other arithmetic, span_part(): face_sum = upwind + downwind  8.71 us
    ppermute x3, starting transfers between devices, padded(): lax.ppermute(lax.slice_in_dim(block, block.shape[dim] - width, None, axis...  7.2 us
    add x2, other arithmetic, face_difference(): face_sum = upwind + downwind  4.5 us
    unnamed x87, local copies, waits for them, and re-layouts  3.51 us
  transfers between devices with their start and end apart: 6, of which 0 were waited for; matrix products, arithmetic and copies ran while one was open for 53% of the time, Pallas kernels for 0%

profile of v1, /device:TPU:8, one launch (start us, length us, event | category | flops | bytes accessed | tf_op | source)
XLA Modules:
  0.0 116.3 jit_solution(14633035460589712181)
XLA Ops:
  0.7 0.8 fusion.104
  1.5 3.4 %collective-permute-start.2 = (f32[3,32]{1,0:T(4,128)S(1)}, f32[3,32]{1,0:T(4,128)S(1)}, u32[]{:S(2)}, u32[]{:S(2)}) collective-permute-start(f32[3,32]{1,0:T(4,128)S(1)} %get-tuple-element.71), channel_id=1, source_target_pairs={{0,16},{16,32},{32,48},{48,64},{64,80},{80,96},{96,112},{112,128},... | collective-permute-start | bytes 1160 | tf_op jit(solution)/shard_map/ppermute | solution.py:24
  4.9 4.6 %collective-permute-start.3 = (f32[3,32]{1,0:T(4,128)S(1)}, f32[3,32]{1,0:T(4,128)S(1)}, u32[]{:S(2)}, u32[]{:S(2)}) collective-permute-start(f32[3,32]{1,0:T(4,128)S(1)} %get-tuple-element.72), channel_id=1, source_target_pairs={{16,0},{32,16},{48,32},{64,48},{80,64},{96,80},{112,96},{128,112},... | collective-permute-start | bytes 1160 | tf_op jit(solution)/shard_map/ppermute | solution.py:27
  9.4 2.2 %fusion.97 = (f32[6,3,3072]{2,1,0:T(4,128)}, f32[6,3,3072]{2,1,0:T(4,128)}) fusion(f32[6,16,3072]{2,1,0:T(8,128)} %param.5), kind=kLoop, calls=%fused_computation.217 | loop fusion | bytes 884736 | tf_op jit(solution)/shard_map/slice | solution.py:25
  11.6 1.9 %collective-permute-start = (f32[6,3,3072]{2,1,0:T(4,128)}, f32[6,3,3072]{2,1,0:T(4,128)}, u32[]{:S(2)}, u32[]{:S(2)}) collective-permute-start(f32[6,3,3072]{2,1,0:T(4,128)} %get-tuple-element.50), channel_id=1, source_target_pairs={{0,16},{16,32},{32,48},{48,64},{64,80},{80,96},{96,112},{112,128},... | collective-permute-start | bytes 663560 | tf_op jit(solution)/shard_map/ppermute | solution.py:24
  13.5 6.0 %collective-permute-start.1 = (f32[6,3,3072]{2,1,0:T(4,128)}, f32[6,3,3072]{2,1,0:T(4,128)}, u32[]{:S(2)}, u32[]{:S(2)}) collective-permute-start(f32[6,3,3072]{2,1,0:T(4,128)} %get-tuple-element.51), channel_id=1, source_target_pairs={{16,0},{32,16},{48,32},{64,48},{80,64},{96,80},{112,96},{128,112},... | collective-permute-start | bytes 663560 | tf_op jit(solution)/shard_map/ppermute | solution.py:27
  19.6 0.7 fusion.98
  20.3 1.9 %collective-permute-start.4 = (f32[6,16,96]{2,1,0:T(8,128)}, f32[6,16,96]{2,1,0:T(8,128)}, u32[]{:S(2)}, u32[]{:S(2)}) collective-permute-start(f32[6,16,96]{2,1,0:T(8,128)} %get-tuple-element.53), channel_id=1, source_target_pairs={{0,1},{1,2},{2,3},{3,4},{4,5},{5,6},{6,7},{7,8},{8,9},{9,10},{10,1... | collective-permute-start | bytes 110600 | tf_op jit(solution)/shard_map/ppermute | solution.py:24
  26.3 0.7 copy_bitcast_fusion
  27.8 0.7 tile.39
  28.6 0.7 mul.830
  29.3 1.3 %collective-permute-start.5 = (f32[6,16,96]{2,1,0:T(8,128)}, f32[6,16,96]{2,1,0:T(8,128)}, u32[]{:S(2)}, u32[]{:S(2)}) collective-permute-start(f32[6,16,96]{2,1,0:T(8,128)} %get-tuple-element.52), channel_id=1, source_target_pairs={{1,0},{2,1},{3,2},{4,3},{5,4},{6,5},{7,6},{8,7},{9,8},{10,9},{11,1... | collective-permute-start | bytes 110600 | tf_op jit(solution)/shard_map/ppermute | solution.py:27
  33.4 1.1 tile.92
  34.5 1.0 tile.93
  35.5 1.5 %fusion.79 = (f32[16,32]{1,0:T(8,128)S(1)}, f32[16,32]{1,0:T(8,128)}, f32[16,32]{1,0:T(8,128)}) fusion(f32[6,16,3072]{2,1,0:T(8,128)S(1)} %copy-done, pred[]{:T(512)S(6)} %eq.69, f32[22,32]{1,0:T(8,128)S(1)} %fusion.56, f32[16,2]{1,0:T(8,128)} %get-tuple-element.62, f32[16,30]{1,0:T(8,128)} %get-tuple-element.64, f32[16,1]{1,0:T(8,128)} %get-tuple-element.66, ...), kind=kLoop, calls=%fused_computation.193 | loop fusion | flops 26624 | bytes 34817 | tf_op jit(solution)/shard_map/jit(_where)/select_n | solution.py:34
  37.0 22.7 %all-gather = f32[256,32]{1,0:T(8,128)S(1)} all-gather(f32[16,32]{1,0:T(8,128)S(1)} %get-tuple-element.12), channel_id=2, replica_groups=mesh['gx'=16,'gy'=16] {'gy'}, dimensions={0}, use_global_device_ids=true | all-gather | bytes 34816 | tf_op jit(solution)/shard_map/all_gather | solution.py:34
  60.4 0.7 tile.94
  61.1 1.1 tile.95
  62.2 1.1 multiply_dynamic-update-slice_fusion.7
  63.4 0.9 broadcast_multiply_fusion.3
  64.9 1.8 %fusion.85 = (f32[6,16,3041]{2,1,0:T(8,128)}, f32[6,16,3041]{2,1,0:T(8,128)}) fusion(f32[6,16,3072]{2,1,0:T(8,128)S(1)} %get-tuple-element.19), kind=kLoop, calls=%fused_computation.205 | loop fusion | bytes 4670976 | tf_op jit(solution)/shard_map/jit(_roll_static)/slice | solution.py:49
  66.7 1.8 %fusion.86 = (f32[6,16,3071]{2,1,0:T(8,128)}, f32[6,16,3071]{2,1,0:T(8,128)}) fusion(f32[6,16,3072]{2,1,0:T(8,128)S(1)} %get-tuple-element.19), kind=kLoop, calls=%fused_computation.206 | loop fusion | bytes 4717056 | tf_op jit(solution)/shard_map/jit(_roll_static)/slice | solution.py:48
  68.5 1.8 %fusion.89 = (f32[6,16,3042]{2,1,0:T(8,128)}, f32[6,16,3042]{2,1,0:T(8,128)}) fusion(f32[6,16,3072]{2,1,0:T(8,128)S(1)} %get-tuple-element.20), kind=kLoop, calls=%fused_computation.209 | loop fusion | bytes 4672512 | tf_op jit(solution)/shard_map/jit(_roll_static)/slice | solution.py:49
  70.3 1.8 %fusion.90 = (f32[6,16,3070]{2,1,0:T(8,128)}, f32[6,16,3070]{2,1,0:T(8,128)}) fusion(f32[6,16,3072]{2,1,0:T(8,128)S(1)} %get-tuple-element.20), kind=kLoop, calls=%fused_computation.210 | loop fusion | bytes 4715520 | tf_op jit(solution)/shard_map/jit(_roll_static)/slice | solution.py:48
  72.1 1.9 %fusion.93 = (f32[6,16,3041]{2,1,0:T(8,128)}, f32[6,16,3041]{2,1,0:T(8,128)}) fusion(f32[6,16,3072]{2,1,0:T(8,128)S(1)} %get-tuple-element.20), kind=kLoop, calls=%fused_computation.213 | loop fusion | bytes 4670976 | tf_op jit(solution)/shard_map/jit(_roll_static)/slice | solution.py:49
  74.0 1.8 %fusion.94 = (f32[6,16,3071]{2,1,0:T(8,128)}, f32[6,16,3071]{2,1,0:T(8,128)}) fusion(f32[6,16,3072]{2,1,0:T(8,128)S(1)} %get-tuple-element.20), kind=kLoop, calls=%fused_computation.214 | loop fusion | bytes 4717056 | tf_op jit(solution)/shard_map/jit(_roll_static)/slice | solution.py:48
  75.8 1.4 %slice.663 = f32[6,16,3070]{2,1,0:T(8,128)} slice(f32[6,16,3072]{2,1,0:T(8,128)S(1)} %get-tuple-element.19), slice={[0:6], [0:16], [2:3072]} | slice | bytes 2357760 | tf_op jit(solution)/shard_map/jit(_roll_static)/slice | solution.py:48
  77.2 1.4 %slice.667 = f32[6,16,3069]{2,1,0:T(8,128)} slice(f32[6,16,3072]{2,1,0:T(8,128)S(1)} %get-tuple-element.19), slice={[0:6], [0:16], [3:3072]} | slice | bytes 2356992 | tf_op jit(solution)/shard_map/jit(_roll_static)/slice | solution.py:48
  78.6 0.7 fusion.84
  79.3 0.7 fusion.87
  80.0 0.7 fusion.88
  80.7 0.7 fusion.91
  82.1 0.7 fusion.95
  82.8 0.7 slice.665
  84.1 0.7 slice.669
  84.9 1.2 %tile.35 = f32[22,3072]{1,0:T(8,128)} reshape(f32[22,96,32]{2,1,0:T(8,128)S(1)} %tile.34) | data formatting | bytes 540672 | tf_op jit(solution)/shard_map/tile | solution.py:111
  86.1 1.7 %broadcast_multiply_fusion.2 = f32[22,3072]{1,0:T(8,128)} fusion(f32[22,3072]{1,0:T(8,128)} %tile.35, f32[3072]{0:T(1024)S(1)} %copy-done.18), kind=kLoop, calls=%fused_computation.132 | loop fusion | flops 67584 | bytes 552960 | tf_op jit(solution)/shard_map/mul | solution.py:110
  87.9 8.7 %fusion.32 = f32[6,16,3072]{2,1,0:T(8,128)S(1)} fusion(f32[6,16,3070]{2,1,0:T(8,128)} %get-tuple-element.37, f32[6,16,2]{2,1,0:T(8,128)} %get-tuple-element.39, f32[6,16,30]{2,1,0:T(8,128)} %get-tuple-element.33, f32[6,16,3042]{2,1,0:T(8,128)} %get-tuple-element.35, f32[6,16,3071]{2,1,0:T(8,128)} %get-tuple-element.45, f32[6,16,1]{2,1,0:T(8,128)} %get-tuple-element.47, ...), kind=kLoop, calls=%fused_computation.60 | loop fusion | flops 14155776 | bytes 22821888 | tf_op jit(solution)/shard_map/add | solution.py:196
  97.3 1.4 %slice.673 = f32[6,16,3041]{2,1,0:T(8,128)} slice(f32[6,16,3072]{2,1,0:T(8,128)S(1)} %fusion.32), slice={[0:6], [0:16], [31:3072]} | slice | bytes 2335488 | tf_op jit(solution)/shard_map/jit(_roll_static)/slice | solution.py:44
  101.1 0.8 broadcast_select_fusion
  102.6 1.5 %concatenate.126 = f32[6,16,3264]{2,1,0:T(8,128)S(1)} concatenate(f32[6,16,96]{2,1,0:T(8,128)} %broadcast_select_fusion.1, f32[6,16,3072]{2,1,0:T(8,128)S(1)} %copy-done, f32[6,16,96]{2,1,0:T(8,128)S(1)} %broadcast_select_fusion), dimensions={2} | concatenate | bytes 2506752 | tf_op jit(solution)/shard_map/concatenate | solution.py:348
  105.0 2.3 %fusion.13 = f32[6,16,3104]{2,1,0:T(8,128)S(1)} fusion(f32[6,16,3264]{2,1,0:T(8,128)S(1)} %get-tuple-element.18, f32[6,16,3264]{2,1,0:T(8,128)S(1)} %get-tuple-element.17), kind=kLoop, calls=%fused_computation.29 | loop fusion | flops 5959680 | bytes 13111296 | tf_op jit(solution)/shard_map/add | solution.py:88
  107.4 1.4 %fusion.10 = f32[6,22,3072]{2,1,0:T(8,128)S(1)} fusion(f32[6,3,3072]{2,1,0:T(4,128)} %collective-permute-done.1, f32[6,16,3072]{2,1,0:T(8,128)S(1)} %copy-done, f32[6,3,3072]{2,1,0:T(4,128)} %collective-permute-done, f32[6,3072]{1,0:T(8,128)S(1)} %copy-done.15, f32[6,3072]{1,0:T(8,128)S(1)} %copy-done.16, pred[22]{0:T(512)(128)(4,1)S(1)} %copy-done.37, ...), kind=kLoop, calls=%fused_computation.21 | loop fusion | flops 1622016 | bytes 3391532 | tf_op jit(solution)/shard_map/jit(_where)/select_n | solution.py:309
  109.4 0.9 copy-done.9
  110.8 2.2 %fusion.2 = f32[6,17,3072]{2,1,0:T(8,128)S(1)} fusion(f32[6,22,3072]{2,1,0:T(8,128)S(1)} %get-tuple-element.16, f32[6,22,3072]{2,1,0:T(8,128)S(1)} %get-tuple-element.15), kind=kLoop, calls=%fused_computation.3 | loop fusion | flops 6266880 | bytes 13787136 | tf_op jit(solution)/shard_map/add | solution.py:88
  113.1 0.9 fusion.25
  114.1 0.8 copy-done.8
  115.1 1.2 %fusion.45 = f32[6,16,3072]{2,1,0:T(8,128)} fusion(f32[6,16,3072]{2,1,0:T(8,128)S(1)} %copy-done, f32[1,16,3072]{2,1,0:T(8,128)S(1)} %slice_add_fusion, f32[5,16,3072]{2,1,0:T(8,128)S(1)} %slice.675), kind=kLoop, calls=%fused_computation.82 | loop fusion | flops 884736 | bytes 3538944 | tf_op jit(solution)/shard_map/add | solution.py:298
  (161 shorter events, 16.2 us)
Async XLA Ops:
  0.6 21.5 %copy-start.24 = (f32[16,32]{1,0:T(8,128)S(1)}, f32[16,32]{1,0:T(8,128)}, u32[]{:S(2)}) copy-start(f32[16,32]{1,0:T(8,128)} %param.6) | copy-start | bytes 6148
  0.6 18.9 %copy-start = (f32[6,16,3072]{2,1,0:T(8,128)S(1)}, f32[6,16,3072]{2,1,0:T(8,128)}, u32[]{:S(2)}) copy-start(f32[6,16,3072]{2,1,0:T(8,128)} %param.5) | copy-start | bytes 3538948
  1.5 27.8 %collective-permute-start.2 = (f32[3,32]{1,0:T(4,128)S(1)}, f32[3,32]{1,0:T(4,128)S(1)}, u32[]{:S(2)}, u32[]{:S(2)}) collective-permute-start(f32[3,32]{1,0:T(4,128)S(1)} %get-tuple-element.71), channel_id=1, source_target_pairs={{0,16},{16,32},{32,48},{48,64},{64,80},{80,96},{96,112},{112,128},... | collective-permute-start | bytes 1160 | tf_op jit(solution)/shard_map/ppermute | solution.py:24
  4.9 25.7 %collective-permute-start.3 = (f32[3,32]{1,0:T(4,128)S(1)}, f32[3,32]{1,0:T(4,128)S(1)}, u32[]{:S(2)}, u32[]{:S(2)}) collective-permute-start(f32[3,32]{1,0:T(4,128)S(1)} %get-tuple-element.72), channel_id=1, source_target_pairs={{16,0},{32,16},{48,32},{64,48},{80,64},{96,80},{112,96},{128,112},... | collective-permute-start | bytes 1160 | tf_op jit(solution)/shard_map/ppermute | solution.py:27
  11.6 95.7 %collective-permute-start = (f32[6,3,3072]{2,1,0:T(4,128)}, f32[6,3,3072]{2,1,0:T(4,128)}, u32[]{:S(2)}, u32[]{:S(2)}) collective-permute-start(f32[6,3,3072]{2,1,0:T(4,128)} %get-tuple-element.50), channel_id=1, source_target_pairs={{0,16},{16,32},{32,48},{48,64},{64,80},{80,96},{96,112},{112,128},... | collective-permute-start | bytes 663560 | tf_op jit(solution)/shard_map/ppermute | solution.py:24
  13.5 93.8 %collective-permute-start.1 = (f32[6,3,3072]{2,1,0:T(4,128)}, f32[6,3,3072]{2,1,0:T(4,128)}, u32[]{:S(2)}, u32[]{:S(2)}) collective-permute-start(f32[6,3,3072]{2,1,0:T(4,128)} %get-tuple-element.51), channel_id=1, source_target_pairs={{16,0},{32,16},{48,32},{64,48},{80,64},{96,80},{112,96},{128,112},... | collective-permute-start | bytes 663560 | tf_op jit(solution)/shard_map/ppermute | solution.py:27
  20.3 81.6 %collective-permute-start.4 = (f32[6,16,96]{2,1,0:T(8,128)}, f32[6,16,96]{2,1,0:T(8,128)}, u32[]{:S(2)}, u32[]{:S(2)}) collective-permute-start(f32[6,16,96]{2,1,0:T(8,128)} %get-tuple-element.53), channel_id=1, source_target_pairs={{0,1},{1,2},{2,3},{3,4},{4,5},{5,6},{6,7},{7,8},{8,9},{9,10},{10,1... | collective-permute-start | bytes 110600 | tf_op jit(solution)/shard_map/ppermute | solution.py:24
  22.8 65.1 %copy-start.29 = (pred[3072]{0:T(1024)(128)(4,1)}, pred[3072]{0:T(1024)(128)(4,1)S(1)}, u32[]{:S(2)}) copy-start(pred[3072]{0:T(1024)(128)(4,1)S(1)} %get-tuple-element.82) | copy-start | bytes 9220
  25.0 0.7 copy-start.40
  25.0 0.7 copy-start.41
  25.0 0.9 copy-start.35
  25.2 37.0 %copy-start.7 = (f32[1,16,3072]{2,1,0:T(8,128)}, f32[1,16,3072]{2,1,0:T(8,128)S(1)}, u32[]{:S(2)}) copy-start(f32[1,16,3072]{2,1,0:T(8,128)S(1)} %get-tuple-element.3) | copy-start | bytes 589828
  26.2 7.1 %copy-start.22 = (f32[6,16,96]{2,1,0:T(8,128)}, f32[6,16,96]{2,1,0:T(8,128)S(1)}, u32[]{:S(2)}) copy-start(f32[6,16,96]{2,1,0:T(8,128)S(1)} %constant_dynamic-update-slice_fusion) | copy-start | bytes 110596
  26.3 7.1 %copy-start.36 = (pred[22]{0:T(512)(128)(4,1)}, pred[22]{0:T(512)(128)(4,1)S(1)}, u32[]{:S(2)}) copy-start(pred[22]{0:T(512)(128)(4,1)S(1)} %get-tuple-element.73) | copy-start | bytes 70
  26.3 7.1 %copy-start.38 = (pred[22]{0:T(512)(128)(4,1)}, pred[22]{0:T(512)(128)(4,1)S(1)}, u32[]{:S(2)}) copy-start(pred[22]{0:T(512)(128)(4,1)S(1)} %get-tuple-element.74) | copy-start | bytes 70
  29.3 71.3 %collective-permute-start.5 = (f32[6,16,96]{2,1,0:T(8,128)}, f32[6,16,96]{2,1,0:T(8,128)}, u32[]{:S(2)}, u32[]{:S(2)}) collective-permute-start(f32[6,16,96]{2,1,0:T(8,128)} %get-tuple-element.52), channel_id=1, source_target_pairs={{1,0},{2,1},{3,2},{4,3},{5,4},{6,5},{7,6},{8,7},{9,8},{10,9},{11,1... | collective-permute-start | bytes 110600 | tf_op jit(solution)/shard_map/ppermute | solution.py:27
  62.2 1.2 %copy-start.10 = (f32[16,3072]{1,0:T(8,128)S(1)}, f32[16,3072]{1,0:T(8,128)}, u32[]{:S(2)}) copy-start(f32[16,3072]{1,0:T(8,128)} %tile.92) | copy-start | bytes 589828
  62.2 1.2 %copy-start.11 = (f32[16,3072]{1,0:T(8,128)S(1)}, f32[16,3072]{1,0:T(8,128)}, u32[]{:S(2)}) copy-start(f32[16,3072]{1,0:T(8,128)} %tile.95) | copy-start | bytes 589828
  62.2 1.2 %copy-start.17 = (f32[3072]{0:T(1024)S(1)}, f32[3072]{0:T(1024)}, u32[]{:S(2)}) copy-start(f32[3072]{0:T(1024)} %mul.794) | copy-start | bytes 36868
  62.2 1.2 %copy-start.26 = (f32[3072]{0:T(1024)S(1)}, f32[3072]{0:T(1024)}, u32[]{:S(2)}) copy-start(f32[3072]{0:T(1024)} %mul.943) | copy-start | bytes 36868
  63.3 1.2 %copy-start.5 = (f32[16,3072]{1,0:T(8,128)}, f32[16,3072]{1,0:T(8,128)S(1)}, u32[]{:S(2)}) copy-start(f32[16,3072]{1,0:T(8,128)S(1)} %get-tuple-element.23) | copy-start | bytes 589828
  63.4 1.2 %copy-start.3 = (f32[6,16,3072]{2,1,0:T(8,128)}, f32[6,16,3072]{2,1,0:T(8,128)S(1)}, u32[]{:S(2)}) copy-start(f32[6,16,3072]{2,1,0:T(8,128)S(1)} %multiply_dynamic-update-slice_fusion.6) | copy-start | bytes 3538948
  64.3 0.7 copy-start.6
  84.8 1.3 %copy-start.18 = (f32[3072]{0:T(1024)S(1)}, f32[3072]{0:T(1024)}, u32[]{:S(2)}) copy-start(f32[3072]{0:T(1024)} %mul.794) | copy-start | bytes 36868
  84.9 3.0 %copy-start.31 = (pred[3072]{0:T(1024)(128)(4,1)S(1)}, pred[3072]{0:T(1024)(128)(4,1)}, u32[]{:S(2)}) copy-start(pred[3072]{0:T(1024)(128)(4,1)} %get-tuple-element.81) | copy-start | bytes 9220
  84.9 3.0 %copy-start.32 = (pred[3072]{0:T(1024)(128)(4,1)S(1)}, pred[3072]{0:T(1024)(128)(4,1)}, u32[]{:S(2)}) copy-start(pred[3072]{0:T(1024)(128)(4,1)} %get-tuple-element.79) | copy-start | bytes 9220
  84.9 2.9 %copy-start.33 = (pred[3072]{0:T(1024)(128)(4,1)S(1)}, pred[3072]{0:T(1024)(128)(4,1)}, u32[]{:S(2)}) copy-start(pred[3072]{0:T(1024)(128)(4,1)} %get-tuple-element.80) | copy-start | bytes 9220
  84.9 2.9 %copy-start.34 = (pred[3072]{0:T(1024)(128)(4,1)S(1)}, pred[3072]{0:T(1024)(128)(4,1)}, u32[]{:S(2)}) copy-start(pred[3072]{0:T(1024)(128)(4,1)} %fusion.63) | copy-start | bytes 9220
  87.9 8.7 %copy-start.21 = (f32[16,32]{1,0:T(8,128)S(1)}, f32[16,32]{1,0:T(8,128)}, u32[]{:S(2)}) copy-start(f32[16,32]{1,0:T(8,128)} %reduce_sum.29) | copy-start | bytes 6148
  87.9 8.7 %copy-start.25 = (f32[16,32]{1,0:T(8,128)S(1)}, f32[16,32]{1,0:T(8,128)}, u32[]{:S(2)}) copy-start(f32[16,32]{1,0:T(8,128)} %param.6) | copy-start | bytes 6148
  96.6 2.1 %copy-start.1 = (f32[6,16,3072]{2,1,0:T(8,128)}, f32[6,16,3072]{2,1,0:T(8,128)S(1)}, u32[]{:S(2)}) copy-start(f32[6,16,3072]{2,1,0:T(8,128)S(1)} %fusion.32) | copy-start | bytes 3538948
  99.3 0.7 copy-start.28
  99.6 0.7 copy-start.27
  100.3 0.8 copy-start.20
  100.3 1.6 %copy-start.23 = (f32[6,16,96]{2,1,0:T(8,128)S(1)}, f32[6,16,96]{2,1,0:T(8,128)}, u32[]{:S(2)}) copy-start(f32[6,16,96]{2,1,0:T(8,128)} %copy-done.22) | copy-start | bytes 110596
  102.5 1.5 %copy-start.14 = (f32[3264]{0:T(1024)S(1)}, f32[3264]{0:T(1024)}, u32[]{:S(2)}) copy-start(f32[3264]{0:T(1024)} %mul.830) | copy-start | bytes 39172
  105.0 2.3 %copy-start.15 = (f32[6,3072]{1,0:T(8,128)S(1)}, f32[6,3072]{1,0:T(8,128)}, u32[]{:S(2)}) copy-start(f32[6,3072]{1,0:T(8,128)} %get-tuple-element.77) | copy-start | bytes 221188
  105.0 2.3 %copy-start.16 = (f32[6,3072]{1,0:T(8,128)S(1)}, f32[6,3072]{1,0:T(8,128)}, u32[]{:S(2)}) copy-start(f32[6,3072]{1,0:T(8,128)} %get-tuple-element.78) | copy-start | bytes 221188
  105.0 2.3 %copy-start.37 = (pred[22]{0:T(512)(128)(4,1)S(1)}, pred[22]{0:T(512)(128)(4,1)}, u32[]{:S(2)}) copy-start(pred[22]{0:T(512)(128)(4,1)} %copy-done.36) | copy-start | bytes 70
  105.0 2.3 %copy-start.39 = (pred[22]{0:T(512)(128)(4,1)S(1)}, pred[22]{0:T(512)(128)(4,1)}, u32[]{:S(2)}) copy-start(pred[22]{0:T(512)(128)(4,1)} %copy-done.38) | copy-start | bytes 70
  107.4 1.5 %copy-start.19 = (f32[3072]{0:T(1024)S(1)}, f32[3072]{0:T(1024)}, u32[]{:S(2)}) copy-start(f32[3072]{0:T(1024)} %mul.794) | copy-start | bytes 36868
  109.3 1.0 copy-start.9
  110.7 2.3 %copy-start.2 = (f32[6,16,3072]{2,1,0:T(8,128)S(1)}, f32[6,16,3072]{2,1,0:T(8,128)}, u32[]{:S(2)}) copy-start(f32[6,16,3072]{2,1,0:T(8,128)} %copy-done.1) | copy-start | bytes 3538948
  110.8 2.3 %copy-start.4 = (f32[6,16,3041]{2,1,0:T(8,128)S(1)}, f32[6,16,3041]{2,1,0:T(8,128)}, u32[]{:S(2)}) copy-start(f32[6,16,3041]{2,1,0:T(8,128)} %slice.673) | copy-start | bytes 3503236
  110.8 2.3 %copy-start.12 = (f32[16,3072]{1,0:T(8,128)S(1)}, f32[16,3072]{1,0:T(8,128)}, u32[]{:S(2)}) copy-start(f32[16,3072]{1,0:T(8,128)} %get-tuple-element.58) | copy-start | bytes 589828
  110.8 2.3 %copy-start.13 = (f32[16,3072]{1,0:T(8,128)S(1)}, f32[16,3072]{1,0:T(8,128)}, u32[]{:S(2)}) copy-start(f32[16,3072]{1,0:T(8,128)} %get-tuple-element.59) | copy-start | bytes 589828
  110.8 2.3 %copy-start.30 = (pred[3072]{0:T(1024)(128)(4,1)S(1)}, pred[3072]{0:T(1024)(128)(4,1)}, u32[]{:S(2)}) copy-start(pred[3072]{0:T(1024)(128)(4,1)} %copy-done.29) | copy-start | bytes 9220
  114.0 0.9 copy-start.8
